TPU v7x, 32 devices: a whole 2x2x4 slice. The times are simulated.
32 devices in a mesh: groups: 2 (over y), fsdp: 4 (over z), segment: 4 (over x, core).
Axes of the slice: x: 2, y: 2, z: 4, core: 2. Of those that a mesh axis runs over, the one named last changes fastest.
Arguments:
- layer_inputs: bfloat16 [32, 8192], P(('groups', 'fsdp'), 'segment'), parts along dimension 0, may hold values from -6 to 6
- labels: int32 [32], P('groups'), parts along dimension 0, may hold values from 0 to 1
- head_weight: float32 [4096], replicated, may hold values from -5 to 5
- gate_up_store: bfloat16 [1280, 4, 2, 128, 128], P('fsdp', 'segment'), may hold values from -0.125 to 0.125
- down_store: bfloat16 [1280, 4, 128, 128], P('fsdp', 'segment'), may hold values from -0.0625 to 0.0625
- kept_rows: int32 [2, 128, 16], replicated, may hold values from 0 to 31, as said below
- owners: int32 [2, 128, 16], replicated, may hold values from 0 to 3, as said below
- slots: int32 [2, 128, 16], replicated, may hold values from 0 to 319, as said below
Outputs:
- input_grads: bfloat16 [32, 8192], P(('groups', 'fsdp'), 'segment'), parts along dimension 0
- gate_up_grads: bfloat16 [2560, 4, 2, 128, 128], P(('groups', 'fsdp'), 'segment'), parts along dimension 0
- down_grads: bfloat16 [2560, 4, 128, 128], P(('groups', 'fsdp'), 'segment'), parts along dimension 0
There are 2 independent parts, one for each index of `groups`. A program takes and returns all parts, laid end to end along the dimension named above; an argument that names none is the same for every part. Nothing has to cross between parts.
Inputs may be any that keep to these rules, and one draw needn't show every extreme that they name: kept_rows[p, j] holds 16 distinct block rows. `owners`: call (j // 16) mod 4 the reader of hidden block column j. For each segment p and each value of j // 64, one fsdp index stores at most 320 of those kept blocks, and at most 80 of them with one reader; both bounds are reached. Kept blocks with the same segment, the same j // 64 and the same owner have distinct slots.
All inputs are finite; a program needn't handle non-finite values.
Results may differ from a plain program's by a relative error of at most 0.008.
Values may be sent and summed in bfloat16 or wider, within the bound.
No kernel may reach another device: no remote copies, remote signals or barrier semaphores. Data moves between devices by JAX's collectives and lax.ppermute only.
A program may use at most 256 MiB of HBM per device.

v0:
```python
import jax
import jax.numpy as jnp
from jax import lax
from jax.sharding import PartitionSpec as P

PIPE = 2


def swapped(x, axis, stride):
    return lax.ppermute(x, axis, [(i, i ^ 1 << stride) for i in range(lax.axis_size(axis))])


def from_behind(block, axis, distance):
    devices = range(lax.axis_size(axis))
    route = [(i - distance, i) for i in devices if i - distance in devices]
    return lax.ppermute(block, axis, route)


def block_trade(first, second):
    return (
        lax.all_to_all(first, "fsdp", split_axis=0, concat_axis=0, tiled=True),
        lax.all_to_all(second, "fsdp", split_axis=0, concat_axis=0, tiled=True),
    )


def gather_whole(share, section, levels):
    current = share
    for level in range(levels):
        other = swapped(current, "segment", level)
        upper = section >> level & 1 == 1
        joined_high = jnp.concatenate([other, current], axis=1)
        joined_low = jnp.concatenate([current, other], axis=1)
        current = jnp.where(upper, joined_high, joined_low)
    return lax.all_gather(current, "fsdp", axis=0, tiled=True)


def reduce_share(partial_value, section, levels):
    current = partial_value
    for level in reversed(range(levels)):
        half = current.shape[1] // 2
        lower = current[:, :half]
        higher = current[:, half:]
        upper = section >> level & 1 == 1
        outgoing = jnp.where(upper, lower, higher)
        staying = jnp.where(upper, higher, lower)
        current = staying + swapped(outgoing, "segment", level)
    return lax.psum_scatter(current, "fsdp", scatter_dimension=0, tiled=True)


def per_device(
    layer_inputs, labels, head_weight, gate_up_store, down_store, kept_rows, owners, slots
):
    members = lax.axis_size("fsdp")
    sections = lax.axis_size("segment") // PIPE
    levels = sections.bit_length() - 1
    member = lax.axis_index("fsdp")
    place = lax.axis_index("segment")
    segment = place // sections
    section = place % sections
    tok_rows, piece_width = layer_inputs.shape
    width = piece_width * sections
    tokens = tok_rows * members
    blk = gate_up_store.shape[-1]
    capacity = gate_up_store.shape[0]
    kept = kept_rows.shape[2]
    ncols = kept_rows.shape[1] // (members * sections)
    reach = ncols * kept
    pairs = (capacity + members - 1) // members
    nrow = width // blk
    is_last = segment == PIPE - 1
    first_col = section * members * ncols
    sec_owner = lax.dynamic_slice(
        owners, (segment, first_col, 0), (1, members * ncols, kept)
    ).reshape(members, reach)
    sec_slot = lax.dynamic_slice(
        slots, (segment, first_col, 0), (1, members * ncols, kept)
    ).reshape(members, reach)
    mine = sec_owner == member
    ranks = jnp.cumsum(mine.astype(jnp.int32), axis=1) - 1
    hits = mine[:, None, :] & (
        ranks[:, None, :] == jnp.arange(pairs, dtype=jnp.int32)[None, :, None]
    )
    picks = jnp.sum(jnp.where(hits, sec_slot[:, None, :], 0), axis=2)
    valid = jnp.any(hits, axis=2)
    store_pair = gate_up_store[:, 0]
    store_down = down_store[:, 0]
    zero_bf = jnp.zeros((), jnp.bfloat16)
    send_pair = jnp.where(valid[:, :, None, None, None], store_pair[picks], zero_bf)
    send_down = jnp.where(valid[:, :, None, None], store_down[picks], zero_bf)
    recv_pair, recv_down = block_trade(send_pair, send_down)
    my_owner = lax.dynamic_index_in_dim(sec_owner, member, 0, keepdims=False)
    entries = jnp.arange(reach, dtype=jnp.int32)
    earlier = jnp.sum(
        ((my_owner[None, :] == my_owner[:, None]) & (entries[None, :] < entries[:, None])).astype(
            jnp.int32
        ),
        axis=1,
    )
    spots = my_owner * pairs + earlier
    w_pair = recv_pair.reshape(members * pairs, 2, blk, blk)[spots].reshape(
        ncols, kept, 2, blk, blk
    )
    w_down = recv_down.reshape(members * pairs, blk, blk)[spots].reshape(ncols, kept, blk, blk)
    my_rows = lax.dynamic_slice(
        kept_rows, (segment, first_col + member * ncols, 0), (1, ncols, kept)
    ).reshape(reach)
    inputs = gather_whole(layer_inputs, section, levels)
    picked = inputs.reshape(tokens, nrow, blk)[:, my_rows, :].reshape(tokens, ncols, kept, blk)
    w_gate = w_pair[:, :, 0]
    w_up = w_pair[:, :, 1]
    gate = jnp.einsum("mikb,ikbc->mic", picked, w_gate, preferred_element_type=jnp.float32)
    up = jnp.einsum("mikb,ikbc->mic", picked, w_up, preferred_element_type=jnp.float32)
    hidden = (jax.nn.silu(gate) * up).astype(jnp.bfloat16)
    head_rows = head_weight.reshape(nrow, blk)[my_rows].reshape(ncols, kept, blk)
    folded = jnp.einsum(
        "ikcd,ikd->ic", w_down.astype(jnp.float32), head_rows, precision=lax.Precision.HIGHEST
    )
    branch = jnp.einsum(
        "mic,ic->m", hidden.astype(jnp.float32), folded, precision=lax.Precision.HIGHEST
    )
    own_head = lax.dynamic_slice_in_dim(head_weight, section * piece_width, piece_width)
    own_term = jnp.dot(layer_inputs.astype(jnp.float32), own_head, precision=lax.Precision.HIGHEST)
    own_full = lax.dynamic_update_slice_in_dim(
        jnp.zeros((tokens,), jnp.float32), own_term, member * tok_rows, 0
    )
    pieces = jnp.where(is_last, branch + own_full, jnp.zeros((tokens,), jnp.float32))
    logits = lax.psum(pieces, ("fsdp", "segment")) * width ** (-0.5)
    dlogit = jax.nn.sigmoid(logits) - labels.astype(jnp.float32)
    dout_last = (dlogit[:, None] * head_weight[None, :]).astype(jnp.bfloat16)
    onehot = (my_rows[:, None] == jnp.arange(nrow, dtype=jnp.int32)[None, :]).astype(jnp.float32)

    def backward(cotangent):
        dpicked = cotangent.reshape(tokens, nrow, blk)[:, my_rows, :].reshape(
            tokens, ncols, kept, blk
        )
        dhidden = jnp.einsum("mikd,ikcd->mic", dpicked, w_down, preferred_element_type=jnp.float32)
        sig = jax.nn.sigmoid(gate)
        dgate = (dhidden * up * sig * (1.0 + gate * (1.0 - sig))).astype(jnp.bfloat16)
        dup = (dhidden * gate * sig).astype(jnp.bfloat16)
        grad_down = jnp.einsum(
            "mic,mikd->ikcd", hidden, dpicked, preferred_element_type=jnp.float32
        ).astype(jnp.bfloat16)
        grad_gate = jnp.einsum(
            "mikb,mic->ikbc", picked, dgate, preferred_element_type=jnp.float32
        ).astype(jnp.bfloat16)
        grad_up = jnp.einsum(
            "mikb,mic->ikbc", picked, dup, preferred_element_type=jnp.float32
        ).astype(jnp.bfloat16)
        spread = jnp.einsum("mic,ikbc->mikb", dgate, w_gate, preferred_element_type=jnp.float32)
        spread = spread + jnp.einsum(
            "mic,ikbc->mikb", dup, w_up, preferred_element_type=jnp.float32
        )
        partial_value = jnp.einsum(
            "sgl,go->sol",
            spread.reshape(tokens, reach, blk),
            onehot,
            precision=lax.Precision.HIGHEST,
        )
        return (
            partial_value.reshape(tokens, width),
            jnp.stack([grad_gate, grad_up], axis=2),
            grad_down,
        )

    def nothing(cotangent):
        return (
            jnp.zeros((tokens, width), jnp.float32),
            jnp.zeros((ncols, kept, 2, blk, blk), jnp.bfloat16),
            jnp.zeros((ncols, kept, blk, blk), jnp.bfloat16),
        )

    rows_at = member * tok_rows
    cols_at = section * piece_width
    part_last, pair_last, down_last = lax.cond(is_last, backward, nothing, dout_last)
    sums_last = reduce_share(part_last, section, levels)
    own_last = lax.dynamic_slice(dout_last, (rows_at, cols_at), (tok_rows, piece_width))
    grad_last = (own_last.astype(jnp.float32) + sums_last).astype(jnp.bfloat16)
    handed = from_behind(grad_last, "segment", -sections)
    dout_first = gather_whole(handed, section, levels)
    part_first, pair_first, down_first = lax.cond(segment == 0, backward, nothing, dout_first)
    sums_first = reduce_share(part_first, section, levels)
    own_first = lax.dynamic_slice(dout_first, (rows_at, cols_at), (tok_rows, piece_width))
    grad_first = (own_first.astype(jnp.float32) + sums_first).astype(jnp.bfloat16)
    input_grads = jnp.where(is_last, grad_last, grad_first)
    block_pair = jnp.where(is_last, pair_last, pair_first).reshape(reach, 2, blk, blk)
    block_down = jnp.where(is_last, down_last, down_first).reshape(reach, blk, blk)
    out_pair = jnp.zeros((members * pairs, 2, blk, blk), jnp.bfloat16).at[spots].set(block_pair)
    out_down = jnp.zeros((members * pairs, blk, blk), jnp.bfloat16).at[spots].set(block_down)
    back_pair, back_down = block_trade(
        out_pair.reshape(members, pairs, 2, blk, blk), out_down.reshape(members, pairs, blk, blk)
    )
    keep_pair = jnp.where(valid[:, :, None, None, None], back_pair, zero_bf).reshape(
        members * pairs, 2, blk, blk
    )
    keep_down = jnp.where(valid[:, :, None, None], back_down, zero_bf).reshape(
        members * pairs, blk, blk
    )
    flat_picks = picks.reshape(members * pairs)
    grads_pair = jnp.zeros((capacity, 2, blk, blk), jnp.bfloat16).at[flat_picks].add(keep_pair)
    grads_down = jnp.zeros((capacity, blk, blk), jnp.bfloat16).at[flat_picks].add(keep_down)
    return (input_grads, grads_pair[:, None], grads_down[:, None])


def solution(mesh):
    return jax.shard_map(
        per_device,
        mesh=mesh,
        in_specs=(
            P(("groups", "fsdp"), "segment"),
            P("groups"),
            P(),
            P("fsdp", "segment", None, None, None),
            P("fsdp", "segment", None, None),
            P(),
            P(),
            P(),
        ),
        out_specs=(
            P(("groups", "fsdp"), "segment"),
            P(("groups", "fsdp"), "segment", None, None, None),
            P(("groups", "fsdp"), "segment", None, None),
        ),
        check_vma=False,
    )
```

profile of v0, /device:TPU:1, one launch (start us, length us, event | category | flops | bytes accessed | tf_op | source)
XLA Modules:
  0.0 1845.3 jit_solution(9677816483919963623)
XLA Ops:
  10.7 14.7 gather_fusion.5
  25.4 10.0 broadcast_select_fusion.4
  41.4 18.4 gather_fusion.2
  59.8 17.4 broadcast_select_fusion.1
  77.2 192.6 %all-to-all-done.1 = bf16[4,80,128,128]{3,2,1,0:T(8,128)(2,1)} async-done(((bf16[4,80,128,128]{3,2,1,0:T(8,128)(2,1)}), bf16[4,80,128,128]{3,2,1,0:T(8,128)(2,1)}, u32[]{:S(2)}, u32[]{:S(2)}) %all-to-all-start.1) | async-done | bytes 10485792 | tf_op jit(solution)/shard_map/all_to_all | solution.py:22
  269.8 7.7 all-to-all-start
  280.3 453.8 %all-gather = bf16[4,4,4096]{2,1,0:T(4,128)(2,1)S(1)} all-gather(bf16[1,4,4096]{2,1,0:T(4,128)(2,1)S(1)} %fusion.22), channel_id=1, replica_groups=mesh['groups'=2,'fsdp'=4,'segment'=4] {'fsdp'}, dimensions={0}, use_global_device_ids=true | all-gather | bytes 163840 | tf_op jit(solution)/shard_map/all_gather | solution.py:34
  735.1 12.8 gather_fusion.6
  747.9 8.9 convolution_bitcast_fusion.4
  756.8 16.8 gather_fusion.3
  773.6 8.1 copy.71
  788.5 11.9 slice_bitcast_fusion
  800.3 32.3 %psum.7 = f32[16]{0:T(128)S(1)} all-reduce(f32[16]{0:T(128)S(1)} %broadcast_select_fusion.8), channel_id=1, replica_groups=mesh['groups'=2,'fsdp'=4,'segment'=4] {'fsdp','segment'}, use_global_device_ids=true, to_apply=%region_5.6 | all-reduce | flops 16 | bytes 128 | tf_op jit(solution)/shard_map/psum | solution.py:127
  832.8 12.2 conditional.2
  848.8 54.0 %all-reduce.5.cloned.1.call-done = f32[16,2048]{1,0:T(8,128)} async-done(((f32[16,2048]{1,0:T(8,128)}), f32[16,2048]{1,0:T(8,128)}) %all-reduce.5.cloned.1.call-update) | async-done | bytes 131088
  912.9 10.5 all-gather.1
  923.4 37.1 %conditional.3 = (bf16[16,16,2,128,128]{3,4,1,0,2:T(8,128)(2,1)}, bf16[16,16,128,128]{2,3,1,0:T(8,128)(2,1)S(1)}, f32[16,2048]{1,0:T(8,128)S(1)}, f32[16,2048]{1,0:T(8,128)S(1)}) conditional(s32[]{:T(128)} %convert_element_type.112, () %tuple.38, (bf16[16,4096]{1,0:T(8,128)(2,1)S(1)}, s32[256]{0:T(256)S(1)}, bf16[16,16,128,128]{3,2,1,0:T(8,128)(2,1)}, ...), branch_computations={%region_9.10_spmd, %region_10.11_spmd} | conditional | flops 1028556544 | bytes 151232640 | solution.py:180
  938.1 12.7 pad_maximum_fusion.1
  964.4 12.3 copy.76
  983.4 36.8 %scatter_fusion.2 = bf16[320,128,128]{2,1,0:T(8,128)(2,1)} fusion(bf16[320,128,128]{2,1,0:T(8,128)(2,1)} %broadcast.198.clone, s32[256]{0:T(256)S(1)} %bitcast.254, bf16[256,128,128]{2,1,0:T(8,128)(2,1)} %bitcast.233), kind=kCustom, calls=%fused_computation.10 | custom fusion | bytes 25166848 | tf_op jit(solution)/shard_map/scatter | solution.py:188
  1026.2 14.1 broadcast_select_fusion.2
  1040.4 21.6 %copy.75 = bf16[16,16,2,128,128]{4,3,2,1,0:T(8,128)(2,1)} copy(bf16[16,16,2,128,128]{3,4,1,0,2:T(8,128)(2,1)} %broadcast_select_fusion.2) | data formatting | bytes 33554432 | tf_op jit(solution)/shard_map/jit(_where)/select_n | solution.py:185
  1061.9 7.6 broadcast.195.clone
  1069.6 44.7 %scatter_fusion = bf16[320,2,128,128]{3,2,1,0:T(8,128)(2,1)} fusion(bf16[320,2,128,128]{3,2,1,0:T(8,128)(2,1)} %broadcast.195.clone, s32[256]{0:T(256)S(1)} %bitcast.255, bf16[256,2,128,128]{3,2,1,0:T(8,128)(2,1)} %bitcast.229), kind=kCustom, calls=%fused_computation.8 | custom fusion | bytes 50332672 | tf_op jit(solution)/shard_map/scatter | solution.py:187
  1114.3 139.4 %all-to-all-done.3 = bf16[4,80,128,128]{3,2,1,0:T(8,128)(2,1)} async-done(((bf16[4,80,128,128]{3,2,1,0:T(8,128)(2,1)}), bf16[4,80,128,128]{3,2,1,0:T(8,128)(2,1)}, u32[]{:S(2)}, u32[]{:S(2)}) %all-to-all-start.3) | async-done | bytes 10485792 | tf_op jit(solution)/shard_map/all_to_all | solution.py:22
  1253.7 7.8 all-to-all-start.2
  1265.0 140.2 %all-reduce.7.cloned.1.call-done = f32[16,2048]{1,0:T(8,128)} async-done(((f32[16,2048]{1,0:T(8,128)}), f32[16,2048]{1,0:T(8,128)}) %all-reduce.7.cloned.1.call-update) | async-done | bytes 131088
  1406.8 10.1 broadcast_select_fusion.3
  1423.6 65.3 %scatter_fusion.3 = bf16[320,128,128]{2,1,0:T(8,128)(2,1)} fusion(bf16[320,128,128]{2,1,0:T(8,128)(2,1)} %broadcast.198, s32[320]{0:T(512)S(1)} %fusion.28, bf16[320,128,128]{2,1,0:T(8,128)(2,1)} %bitcast.230), kind=kCustom, calls=%fused_computation.11 | custom fusion | flops 5242880 | bytes 31458560 | tf_op jit(solution)/shard_map/scatter-add | solution.py:200
  1488.9 229.1 %all-to-all-done.2 = bf16[4,80,2,128,128]{4,3,2,1,0:T(8,128)(2,1)} async-done(((bf16[4,80,2,128,128]{4,3,2,1,0:T(8,128)(2,1)}), bf16[4,80,2,128,128]{4,3,2,1,0:T(8,128)(2,1)}, u32[]{:S(2)}, u32[]{:S(2)}) %all-to-all-start.2) | async-done | bytes 20971552 | tf_op jit(solution)/shard_map/all_to_all | solution.py:21
  1718.0 17.4 broadcast_select_fusion
  1743.1 95.1 %scatter_fusion.1 = bf16[320,2,128,128]{3,2,1,0:T(8,128)(2,1)} fusion(bf16[320,2,128,128]{3,2,1,0:T(8,128)(2,1)} %broadcast.195, s32[320]{0:T(512)S(1)} %fusion.28, bf16[320,2,128,128]{3,2,1,0:T(8,128)(2,1)} %bitcast.214), kind=kCustom, calls=%fused_computation.9 | custom fusion | flops 10485760 | bytes 62915840 | tf_op jit(solution)/shard_map/scatter-add | solution.py:199
  (130 shorter events, 105.0 us)
Async XLA Ops:
  7.2 2.8 copy-start
  10.4 49.4 %copy-start.7 = (pred[4,80]{1,0:T(4,128)(4,1)}, pred[4,80]{1,0:T(4,128)(4,1)S(1)}, u32[]{:S(2)}) copy-start(pred[4,80]{1,0:T(4,128)(4,1)S(1)} %fusion.20) | copy-start | bytes 964
  10.6 14.8 copy-start.4
  35.4 234.5 %all-to-all-start.1 = ((bf16[4,80,128,128]{3,2,1,0:T(8,128)(2,1)}), bf16[4,80,128,128]{3,2,1,0:T(8,128)(2,1)}, u32[]{:S(2)}, u32[]{:S(2)}) async-start(bf16[4,80,128,128]{3,2,1,0:T(8,128)(2,1)} %broadcast_select_fusion.4), calls=%async_computation.1 | async-start | bytes 20971520 | tf_op jit(solution)/shard_map/all_to_all | solution.py:22
  77.2 200.4 %copy-start.6 = (bf16[4,2048]{1,0:T(4,128)(2,1)S(1)}, bf16[4,2048]{1,0:T(4,128)(2,1)}, u32[]{:S(2)}) copy-start(bf16[4,2048]{1,0:T(4,128)(2,1)} %param.12) | copy-start | bytes 49156
  77.2 201.7 %copy-start.9 = (s32[2,128,16]{1,2,0:T(8,128)S(1)}, s32[2,128,16]{1,2,0:T(8,128)}, u32[]{:S(2)}) copy-start(s32[2,128,16]{1,2,0:T(8,128)} %param.17) | copy-start | bytes 49156
  77.2 202.3 %copy-start.2 = (f32[4096]{0:T(1024)S(1)}, f32[4096]{0:T(1024)}, u32[]{:S(2)}) copy-start(f32[4096]{0:T(1024)} %param.14) | copy-start | bytes 49156
  269.8 487.0 %all-to-all-start = ((bf16[4,80,2,128,128]{4,3,2,1,0:T(8,128)(2,1)}), bf16[4,80,2,128,128]{4,3,2,1,0:T(8,128)(2,1)}, u32[]{:S(2)}, u32[]{:S(2)}) async-start(bf16[4,80,2,128,128]{4,3,2,1,0:T(8,128)(2,1)} %broadcast_select_fusion.1), calls=%async_computation | async-start | bytes 41943040 | tf_op jit(solution)/shard_map/all_to_all | solution.py:21
  277.6 625.2 %all-reduce.5.cloned.1.call-start = ((), (), s32[]{:S(2)}) async-start(), calls=%async_computation.4 | async-start | bytes 262144
  277.6 2.6 collective-permute-start
  781.7 6.2 copy-start.3
  788.5 44.1 %copy-start.10 = (s32[16]{0:T(128)S(1)}, s32[16]{0:T(128)}, u32[]{:S(2)}) copy-start(s32[16]{0:T(128)} %param.13) | copy-start | bytes 196
  832.7 14.7 copy-start.11
  844.9 1.8 collective-permute-start.1
  903.7 4.5 collective-permute-start.2
  908.2 4.7 collective-permute-start.3
  932.4 18.3 slice-start.2
  932.4 20.6 %slice-start.6 = ((s8[8388608]{0:T(1024)(128)(4,1)}), s8[4194304]{0:T(1024)(128)(4,1)S(1)}, s32[]{:S(2)}) async-start(s8[8388608]{0:T(1024)(128)(4,1)} %bitcast.223), calls=%async_computation.12 | async-start | bytes 8388608 | tf_op jit(solution)/shard_map/cond
  938.0 12.7 slice-start.3
  938.0 15.0 slice-start.7
  1020.2 233.5 %all-to-all-start.3 = ((bf16[4,80,128,128]{3,2,1,0:T(8,128)(2,1)}), bf16[4,80,128,128]{3,2,1,0:T(8,128)(2,1)}, u32[]{:S(2)}, u32[]{:S(2)}) async-start(bf16[4,80,128,128]{3,2,1,0:T(8,128)(2,1)} %bitcast.216), calls=%async_computation.3 | async-start | bytes 20971520 | tf_op jit(solution)/shard_map/all_to_all | solution.py:22
  1253.7 11.2 copy-start.5
  1253.7 153.0 %copy-start.8 = (pred[4,80]{1,0:T(4,128)(4,1)S(1)}, pred[4,80]{1,0:T(4,128)(4,1)}, u32[]{:S(2)}) copy-start(pred[4,80]{1,0:T(4,128)(4,1)} %copy-done.7) | copy-start | bytes 964
  1253.7 464.3 %all-to-all-start.2 = ((bf16[4,80,2,128,128]{4,3,2,1,0:T(8,128)(2,1)}), bf16[4,80,2,128,128]{4,3,2,1,0:T(8,128)(2,1)}, u32[]{:S(2)}, u32[]{:S(2)}) async-start(bf16[4,80,2,128,128]{4,3,2,1,0:T(8,128)(2,1)} %bitcast.212), calls=%async_computation.2 | async-start | bytes 41943040 | tf_op jit(solution)/shard_map/all_to_all | solution.py:21
  1261.6 143.6 %all-reduce.7.cloned.1.call-start = ((), (), s32[]{:S(2)}) async-start(), calls=%async_computation.5 | async-start | bytes 262144
  1261.7 2.5 collective-permute-start.4
  1743.1 95.1 %copy-start.1 = (s32[2,128,16]{1,2,0:T(8,128)S(1)}, s32[2,128,16]{1,2,0:T(8,128)}, u32[]{:S(2)}) copy-start(s32[2,128,16]{1,2,0:T(8,128)} %param.19) | copy-start | bytes 49156
Sparse Core Ops, SparseCore 0:
  847.6 55.1 all-reduce.4
  1265.4 139.7 all-reduce.6
where the time goes:
time: 1860 us; the launch traced here: 1850 us
  waiting for transfers between devices  761 us (41%)
  blocking collectives  497 us (27%)
  other arithmetic  253 us (14%)
  local copies, waits for them, and re-layouts  247 us (13%)
  starting transfers between devices  36.5 us (2%)
  matrix products  34.7 us (2%)
    all_gather x2, blocking collectives, gather_whole(): return lax.all_gather(current, 'fsdp', axis=0, tiled=True)  464 us
    all_to_all x2, waiting for transfers between devices, block_trade(): lax.all_to_all(second, 'fsdp', split_axis=0, concat_axis=0, tiled=True)  332 us
    all_to_all x2, waiting for transfers between devices, block_trade(): lax.all_to_all(first, 'fsdp', split_axis=0, concat_axis=0, tiled=True)  229 us
    unnamed x4, waiting for transfers between devices  194 us
    scatter-add x1, other arithmetic, per_device(): jnp.zeros((capacity, 2, blk, blk), jnp.bfloat16).at[flat_picks]  95.1 us
    scatter-add x1, other arithmetic, per_device(): jnp.zeros((capacity, blk, blk), jnp.bfloat16).at[flat_picks].add(keep_down)  65.3 us
    scatter x1, local copies, waits for them, and re-layouts, per_device(): jnp.zeros((members * pairs, 2, blk, blk), jnp.bfloat16).at[spots]  44.7 us
    another operation x8, local copies, waits for them, and re-layouts  40.5 us
  transfers between devices with their start and end apart: 11, of which 9 were waited for; matrix products, arithmetic and copies ran while one was open for 13% of the time, Pallas kernels for 0%

commit v1 on v0

v1 whole, which is shorter than its diff:
```python
import jax
import jax.numpy as jnp
from jax import lax
from jax.sharding import PartitionSpec as P

PIPE = 2
HI = lax.Precision.HIGHEST


def per_device(
    layer_inputs, labels, head_weight, gate_up_store, down_store, kept_rows, owners, slots
):
    members = lax.axis_size("fsdp")
    places = lax.axis_size("segment")
    sections = places // PIPE
    member = lax.axis_index("fsdp")
    place = lax.axis_index("segment")
    segment = place // sections
    section = place % sections
    is_last = segment == PIPE - 1
    tok_rows, piece_width = layer_inputs.shape
    tokens = tok_rows * members
    width = piece_width * sections
    blk = gate_up_store.shape[-1]
    capacity = gate_up_store.shape[0]
    kept = kept_rows.shape[2]
    sec_cols = kept_rows.shape[1] // sections
    nrow = width // blk
    nblocks = sec_cols * kept

    first_col = section * sec_cols
    sec_rows = lax.dynamic_slice(kept_rows, (segment, first_col, 0), (1, sec_cols, kept))
    sec_owner = lax.dynamic_slice(owners, (segment, first_col, 0), (1, sec_cols, kept))
    sec_slot = lax.dynamic_slice(slots, (segment, first_col, 0), (1, sec_cols, kept))
    sec_rows = sec_rows.reshape(nblocks)
    mine = sec_owner.reshape(nblocks) == member
    block_col = jnp.arange(nblocks, dtype=jnp.int32) // kept
    hits = mine[None, :] & (
        sec_slot.reshape(nblocks)[None, :] == jnp.arange(capacity, dtype=jnp.int32)[:, None]
    )
    valid = jnp.any(hits, axis=1)
    slot_col = jnp.sum(jnp.where(hits, block_col[None, :], 0), axis=1)
    slot_row = jnp.sum(jnp.where(hits, sec_rows[None, :], 0), axis=1)
    col_hot = valid[:, None] & (slot_col[:, None] == jnp.arange(sec_cols, dtype=jnp.int32)[None, :])
    row_hot = valid[:, None] & (slot_row[:, None] == jnp.arange(nrow, dtype=jnp.int32)[None, :])
    col_f = col_hot.astype(jnp.float32)
    col_b = col_hot.astype(jnp.bfloat16)
    row_f = row_hot.astype(jnp.float32)
    row_b = row_hot.astype(jnp.bfloat16)

    w_pair = gate_up_store[:, 0]
    w_down = down_store[:, 0]

    gathered = lax.all_gather(layer_inputs, ("fsdp", "segment"))
    gathered = gathered.reshape(members, places, tok_rows, piece_width)
    x_all = gathered.transpose(0, 2, 1, 3).reshape(tokens, places * piece_width)
    x_mine = lax.dynamic_slice_in_dim(x_all, segment * width, width, axis=1)
    x_last = x_all[:, (PIPE - 1) * width:]
    x_sel = jnp.einsum("cr,trb->ctb", row_b, x_mine.reshape(tokens, nrow, blk))
    x_sel = x_sel.astype(jnp.bfloat16)

    gu_slot = jnp.einsum("cta,cgab->ctgb", x_sel, w_pair, preferred_element_type=jnp.float32)
    gu_part = jnp.einsum("cj,ctgb->gtjb", col_f, gu_slot, precision=HI)
    head_rows = head_weight.reshape(nrow, blk)
    head_sel = jnp.einsum("cr,rd->cd", row_f, head_rows, precision=HI)
    folded = jnp.einsum(
        "chd,cd->ch", w_down.astype(jnp.float32), head_sel, precision=HI
    )
    f_part = jnp.einsum("cj,ch->jh", col_f, folded, precision=HI)
    packed = jnp.concatenate(
        [gu_part.reshape(2 * tokens, sec_cols, blk), f_part[None]], axis=0
    )
    packed = lax.psum(packed, "fsdp")
    gate = packed[:tokens]
    up = packed[tokens:2 * tokens]
    f_sum = packed[2 * tokens]
    sig = jax.nn.sigmoid(gate)
    hidden = (gate * sig * up).astype(jnp.bfloat16)

    branch = jnp.einsum("tjh,jh->t", hidden.astype(jnp.float32), f_sum, precision=HI)
    branch = jnp.where(is_last, branch, 0.0)
    branch = lax.psum(branch, "segment")
    x_term = jnp.einsum("td,d->t", x_last.astype(jnp.float32), head_weight, precision=HI)
    logits = (x_term + branch) * width ** (-0.5)
    dlogit = jax.nn.sigmoid(logits) - labels.astype(jnp.float32)
    dout_last = (dlogit[:, None] * head_weight[None, :]).astype(jnp.bfloat16)

    def gate_grads(dhidden):
        dgate = (dhidden * up * sig * (1.0 + gate * (1.0 - sig))).astype(jnp.bfloat16)
        dup = (dhidden * gate * sig).astype(jnp.bfloat16)
        pair = jnp.stack([dgate, dup], axis=2)
        return jnp.einsum("cj,tjgb->ctgb", col_b, pair).astype(jnp.bfloat16)

    def spread_rows(d_sel):
        spread = jnp.einsum(
            "ctgb,cgab->cta", d_sel, w_pair, preferred_element_type=jnp.float32
        )
        return jnp.einsum("cr,cta->tra", row_f, spread, precision=HI).reshape(tokens, width)

    d_sel_last = gate_grads(dlogit[:, None, None] * f_sum[None])
    part_last = jnp.where(is_last, spread_rows(d_sel_last), 0.0)
    sum_last = lax.psum(part_last, ("fsdp", "segment"))
    grad_last = (dout_last.astype(jnp.float32) + sum_last).astype(jnp.bfloat16)

    dout_sel = jnp.einsum("cr,trd->ctd", row_b, grad_last.reshape(tokens, nrow, blk))
    dout_sel = dout_sel.astype(jnp.bfloat16)
    dh_slot = jnp.einsum("ctd,chd->cth", dout_sel, w_down, preferred_element_type=jnp.float32)
    dh_part = jnp.einsum("cj,cth->tjh", col_f, dh_slot, precision=HI)
    dhidden_first = lax.psum(dh_part, "fsdp")
    d_sel_first = gate_grads(dhidden_first)
    part_first = jnp.where(is_last, 0.0, spread_rows(d_sel_first))
    sum_first = lax.psum(part_first, ("fsdp", "segment"))
    grad_first = (grad_last.astype(jnp.float32) + sum_first).astype(jnp.bfloat16)

    rows_at = member * tok_rows
    cols_at = section * piece_width
    grads = jnp.where(is_last, grad_last, grad_first)
    input_grads = lax.dynamic_slice(grads, (rows_at, cols_at), (tok_rows, piece_width))

    d_sel = jnp.where(is_last, d_sel_last, d_sel_first)
    cot_sel = jnp.where(
        is_last,
        jnp.einsum("cr,trd->ctd", row_b, dout_last.reshape(tokens, nrow, blk)).astype(
            jnp.bfloat16
        ),
        dout_sel,
    )
    hid_sel = jnp.einsum("cj,tjh->cth", col_b, hidden).astype(jnp.bfloat16)
    grad_pair = jnp.einsum(
        "cta,ctgb->cgab", x_sel, d_sel, preferred_element_type=jnp.float32
    ).astype(jnp.bfloat16)
    grad_down = jnp.einsum(
        "cth,ctd->chd", hid_sel, cot_sel, preferred_element_type=jnp.float32
    ).astype(jnp.bfloat16)
    zero_bf = jnp.zeros((), jnp.bfloat16)
    grad_pair = jnp.where(valid[:, None, None, None], grad_pair, zero_bf)
    grad_down = jnp.where(valid[:, None, None], grad_down, zero_bf)
    return (input_grads, grad_pair[:, None], grad_down[:, None])


def solution(mesh):
    return jax.shard_map(
        per_device,
        mesh=mesh,
        in_specs=(
            P(("groups", "fsdp"), "segment"),
            P("groups"),
            P(),
            P("fsdp", "segment", None, None, None),
            P("fsdp", "segment", None, None),
            P(),
            P(),
            P(),
        ),
        out_specs=(
            P(("groups", "fsdp"), "segment"),
            P(("groups", "fsdp"), "segment", None, None, None),
            P(("groups", "fsdp"), "segment", None, None),
        ),
        check_vma=False,
    )
```

time: 1860 us -> 405 us (0.22)
  waiting for transfers between devices: 761 us -> 209 us
  blocking collectives: 497 us -> 29.5 us
  other arithmetic: 253 us -> 8.74 us
  local copies, waits for them, and re-layouts: 247 us -> 32.3 us
  matrix products: 34.7 us -> 107 us
  starting transfers between devices: 36.5 us -> 0.16 us
    all_to_all x4 -> x0, waiting for transfers between devices: 561 us -> none  [the longest x2 332 us: block_trade(): lax.all_to_all(second, 'fsdp', split_axis=0, concat_axis=0, tiled=True)]
    all_gather x2 -> x1, blocking collectives: 464 us -> 23.9 us  [per_device(): gathered = lax.all_gather(layer_inputs, ('fsdp', 'segment'))]
    psum x0 -> x4, waiting for transfers between devices: none -> 208 us  [the longest x1 87.7 us: per_device(): sum_last = lax.psum(part_last, ('fsdp', 'segment'))]
    unnamed x4, waiting for transfers between devices: 194 us -> 0.07 us
    scatter-add x2 -> x0, other arithmetic: 160 us -> none  [the longest x1 95.1 us: per_device(): jnp.zeros((capacity, 2, blk, blk), jnp.bfloat16).at[flat_picks]]
    scatter x2 -> x0, local copies, waits for them, and re-layouts: 81.6 us -> none  [the longest x1 44.7 us: per_device(): jnp.zeros((members * pairs, 2, blk, blk), jnp.bfloat16).at[spots]]
    gather x8 -> x0, local copies, waits for them, and re-layouts: 73.3 us -> none  [the longest x2 24.9 us: per_device(): recv_pair.reshape(members * pairs, 2, blk, blk)[spots]]
    select_n x15 -> x2, other arithmetic: 74.4 us -> 1.55 us  [the longest x1 1.54 us: per_device(): grads = jnp.where(is_last, grad_last, grad_first)]
  transfers between devices with their start and end apart: 11 -> 4, of which waited for: 9 -> 4; matrix products, arithmetic and copies ran while one was open for 13% -> 15% of each run, Pallas kernels for 0% -> 0%
where the time goes in v1:
time: 405 us; the launch traced here: 401 us
  waiting for transfers between devices  209 us (52%)
  matrix products  107 us (26%)
  local copies, waits for them, and re-layouts  32.3 us (8%)
  blocking collectives  29.5 us (7%)
  between operations  14.3 us (4%)
  other arithmetic  8.74 us (2%)
    psum x1, waiting for transfers between devices, per_device(): sum_last = lax.psum(part_last, ('fsdp', 'segment'))  87.7 us
    psum x1, waiting for transfers between devices, per_device(): packed = lax.psum(packed, 'fsdp')  49.9 us
    psum x1, waiting for transfers between devices, per_device(): sum_first = lax.psum(part_first, ('fsdp', 'segment'))  45.8 us
    unnamed x23, local copies, waits for them, and re-layouts  29.9 us
    psum x1, waiting for transfers between devices, per_device(): dhidden_first = lax.psum(dh_part, 'fsdp')  25 us
    all_gather x1, blocking collectives, per_device(): gathered = lax.all_gather(layer_inputs, ('fsdp', 'segment'))  23.9 us
    dot_general x2, matrix products, spread_rows(): jnp.einsum('ctgb,cgab->cta', d_sel, w_pair, preferred_element_type=jnp.fl...  21.5 us
    dot_general x1, matrix products, per_device(): jnp.einsum('chd,cd->ch', w_down.astype(jnp.float32), head_sel, precision=HI)  19.4 us
  transfers between devices with their start and end apart: 4, of which 4 were waited for; matrix products, arithmetic and copies ran while one was open for 15% of the time, Pallas kernels for 0%

profile of v1, /device:TPU:1, one launch (start us, length us, event | category | flops | bytes accessed | tf_op | source)
XLA Modules:
  0.0 400.9 jit_solution(11632360739966436155)
XLA Ops:
  7.3 0.8 constant_dynamic-slice_fusion
  9.3 23.9 %all-gather.1 = bf16[16,4,2048]{2,1,0:T(4,128)(2,1)S(1)} all-gather(bf16[1,4,2048]{2,1,0:T(4,128)(2,1)} %bitcast.150), channel_id=2, replica_groups=mesh['groups'=2,'fsdp'=4,'segment'=4] {'fsdp','segment'}, dimensions={0}, use_global_device_ids=true | all-gather | bytes 278528 | tf_op jit(solution)/shard_map/all_gather | solution.py:54
  34.6 1.0 fusion.94
  36.2 19.4 %fusion.8 = f32[320,1,128]{2,1,0:T(1,128)S(1)} fusion(f32[320,128,1]{1,2,0:T(1,128)S(1)} %bitcast.141, bf16[320,1,128,128]{3,2,1,0:T(8,128)(2,1)} %param.12), kind=kOutput, calls=%fused_computation.9 | convolution fusion | flops 62914560 | bytes 10813440 | tf_op jit(solution)/shard_map/chd,cd->ch/dot_general | solution.py:66
  55.8 9.1 %fusion.4 = f32[320,16,2,128]{3,1,2,0:T(8,128)S(1)} fusion(bf16[320,1,2,128,128]{4,3,2,1,0:T(8,128)(2,1)} %param.11, bf16[320,16,128,1]{2,0,1,3:T(8,128)(2,1)S(1)} %convolution_bitcast_fusion), kind=kOutput, calls=%fused_computation.4 | convolution fusion | flops 335544320 | bytes 27525120 | tf_op jit(solution)/shard_map/cta,cgab->ctgb/dot_general | solution.py:62
  64.9 5.3 %fusion.31 = f32[2,16,64,128]{3,2,0,1:T(8,128)S(1)} fusion(f32[320,16,2,128]{3,1,2,0:T(8,128)S(1)} %fusion.4, s32[320]{0:T(512)S(1)} %get-tuple-element.15, pred[320]{0:T(512)(128)(4,1)S(1)} %fusion.38), kind=kOutput, calls=%fused_computation.28 | convolution fusion | flops 1006673920 | bytes 6293056 | tf_op jit(solution)/shard_map/cj,ctgb->gtjb/dot_general | solution.py:63
  70.3 1.1 pad_maximum_fusion
  71.5 49.9 %all-reduce.5.cloned.1.call-done = f32[33,64,128]{2,1,0:T(8,128)} async-done(((f32[33,64,128]{2,1,0:T(8,128)}), f32[33,64,128]{2,1,0:T(8,128)}) %all-reduce.5.cloned.1.call-update) | async-done | bytes 1081360 | tf_op jit(solution)/shard_map/psum | solution.py:73
  121.5 0.9 fusion.118
  122.3 1.3 multiply_convert_fusion.2
  124.2 5.6 %psum.36 = f32[16]{0:T(128)S(1)} all-reduce(f32[16]{0:T(128)S(1)} %fusion.50), channel_id=1, replica_groups=mesh['groups'=2,'fsdp'=4,'segment'=4] {'segment'}, use_global_device_ids=true, to_apply=%region_4.5 | all-reduce | flops 16 | bytes 128 | tf_op jit(solution)/shard_map/psum | solution.py:82
  130.4 0.9 fusion.63
  131.3 10.8 %fusion.21 = f32[320,16,128]{2,1,0:T(8,128)S(1)} fusion(bf16[320,1,2,128,128]{4,3,2,1,0:T(8,128)(2,1)} %param.11, bf16[320,16,2,128]{3,0,2,1:T(8,128)(2,1)S(1)} %fusion.63), kind=kOutput, calls=%fused_computation.24 | convolution fusion | flops 335544320 | bytes 26214400 | tf_op jit(solution)/shard_map/ctgb,cgab->cta/dot_general | solution.py:95
  142.1 1.8 fusion.42
  143.8 0.9 copy.136
  144.8 1.6 fusion.81
  146.4 87.7 %all-reduce.7.cloned.1.call-done = f32[16,4096]{1,0:T(8,128)} async-done(((f32[16,4096]{1,0:T(8,128)}), f32[16,4096]{1,0:T(8,128)}) %all-reduce.7.cloned.1.call-update) | async-done | bytes 262160 | tf_op jit(solution)/shard_map/psum | solution.py:102
  234.1 1.0 fusion.126
  235.7 8.7 %fusion.6 = f32[320,16,128]{2,1,0:T(8,128)S(1)} fusion(bf16[320,1,128,128]{3,2,1,0:T(8,128)(2,1)} %param.12, bf16[320,16,128]{2,0,1:T(8,128)(2,1)S(1)} %fusion.114), kind=kOutput, calls=%fused_computation.7 | convolution fusion | flops 167772160 | bytes 14417920 | tf_op jit(solution)/shard_map/ctd,chd->cth/dot_general | solution.py:107
  244.5 2.7 fusion.39
  247.4 2.0 convolution_select_fusion
  249.4 10.1 %select_bitcast_fusion.1 = bf16[320,1,128,128]{3,2,1,0:T(8,128)(2,1)} fusion(pred[320]{0:T(512)(128)(4,1)S(1)} %fusion.38, bf16[320,16,128]{2,0,1:T(8,128)(2,1)S(1)} %convolution_select_fusion, bf16[320,16,128]{2,0,1:T(8,128)(2,1)S(1)} %copy-done.4), kind=kOutput, calls=%fused_computation.11 | convolution fusion | flops 178257920 | bytes 13107520 | tf_op jit(solution)/shard_map/cth,ctd->chd/dot_general | solution.py:132
  259.5 25.0 %all-reduce.9.cloned.1.call-done = f32[16,64,128]{2,1,0:T(8,128)} async-done(((f32[16,64,128]{2,1,0:T(8,128)}), f32[16,64,128]{2,1,0:T(8,128)}) %all-reduce.9.cloned.1.call-update) | async-done | bytes 524304 | tf_op jit(solution)/shard_map/psum | solution.py:109
  284.5 1.6 fusion.69
  286.1 2.4 broadcast_select_fusion
  288.5 10.8 %fusion.26 = f32[320,16,128]{2,1,0:T(8,128)S(1)} fusion(bf16[320,1,2,128,128]{4,3,2,1,0:T(8,128)(2,1)} %param.11, bf16[320,16,2,128]{3,0,2,1:T(8,128)(2,1)S(1)} %get-tuple-element.24), kind=kOutput, calls=%fused_computation.25 | convolution fusion | flops 335544320 | bytes 26214400 | tf_op jit(solution)/shard_map/ctgb,cgab->cta/dot_general | solution.py:95
  299.3 1.8 fusion.45
  301.0 0.9 copy.135
  301.9 16.9 %select_bitcast_fusion = bf16[320,1,2,128,128]{3,4,2,0,1:T(8,128)(2,1)} fusion(pred[320]{0:T(512)(128)(4,1)S(1)} %fusion.38, bf16[320,16,2,128]{3,0,2,1:T(8,128)(2,1)} %get-tuple-element.23, bf16[320,16,128,1]{2,0,1,3:T(8,128)(2,1)S(1)} %copy-done.3), kind=kOutput, calls=%fused_computation.6 | convolution fusion | flops 356515840 | bytes 24904000 | tf_op jit(solution)/shard_map/cta,ctgb->cgab/dot_general | solution.py:129
  318.8 27.9 %copy.71 = bf16[320,1,2,128,128]{4,3,2,1,0:T(8,128)(2,1)} copy(bf16[320,1,2,128,128]{3,4,2,0,1:T(8,128)(2,1)} %select_bitcast_fusion) | data formatting | bytes 41943040
  346.8 45.8 %all-reduce.11.cloned.1.call-done = f32[16,4096]{1,0:T(8,128)} async-done(((f32[16,4096]{1,0:T(8,128)}), f32[16,4096]{1,0:T(8,128)}) %all-reduce.11.cloned.1.call-update) | async-done | bytes 262160 | tf_op jit(solution)/shard_map/psum | solution.py:112
  392.6 1.5 fusion.104
  (47 shorter events, 5.4 us)
Async XLA Ops:
  7.2 114.3 %all-reduce.5.cloned.1.call-start = ((), (), s32[]{:S(2)}) async-start(), calls=%async_computation | async-start | bytes 2162688 | tf_op jit(solution)/shard_map/psum | solution.py:73
  36.2 19.6 %copy-start.2 = (bf16[320,16,128,1]{2,0,1,3:T(8,128)(2,1)}, bf16[320,16,128,1]{2,0,1,3:T(8,128)(2,1)S(1)}, u32[]{:S(2)}) copy-start(bf16[320,16,128,1]{2,0,1,3:T(8,128)(2,1)S(1)} %convolution_bitcast_fusion) | copy-start | bytes 3932164
  70.3 59.5 %copy-start.6 = (f32[4096]{0:T(1024)S(1)}, f32[4096]{0:T(1024)}, u32[]{:S(2)}) copy-start(f32[4096]{0:T(1024)} %param.10) | copy-start | bytes 49156
  70.3 59.5 %copy-start.7 = (s32[16]{0:T(128)S(1)}, s32[16]{0:T(128)}, u32[]{:S(2)}) copy-start(s32[16]{0:T(128)} %param.9) | copy-start | bytes 196
  71.5 162.6 %all-reduce.7.cloned.1.call-start = ((), (), s32[]{:S(2)}) async-start(), calls=%async_computation.1 | async-start | bytes 524288 | tf_op jit(solution)/shard_map/psum | solution.py:102
  121.5 8.6 %copy-start.1 = (f32[33,64,128]{2,1,0:T(8,128)S(1)}, f32[33,64,128]{2,1,0:T(8,128)}, u32[]{:S(2)}) copy-start(f32[33,64,128]{2,1,0:T(8,128)} %all-reduce.5.cloned.1.call-done) | copy-start | bytes 3244036
  144.7 139.8 %all-reduce.9.cloned.1.call-start = ((), (), s32[]{:S(2)}) async-start(), calls=%async_computation.2 | async-start | bytes 1048576 | tf_op jit(solution)/shard_map/psum | solution.py:109
  235.7 8.8 %copy-start = (bf16[320,16,128]{2,0,1:T(8,128)(2,1)}, bf16[320,16,128]{2,0,1:T(8,128)(2,1)S(1)}, u32[]{:S(2)}) copy-start(bf16[320,16,128]{2,0,1:T(8,128)(2,1)S(1)} %fusion.114) | copy-start | bytes 3932164
  244.5 2.8 copy-start.5
  247.2 145.3 %all-reduce.11.cloned.1.call-start = ((), (), s32[]{:S(2)}) async-start(), calls=%async_computation.3 | async-start | bytes 524288 | tf_op jit(solution)/shard_map/psum | solution.py:112
  247.3 2.1 copy-start.4
  299.3 2.7 copy-start.3
Sparse Core Ops, SparseCore 0:
  71.6 49.8 all-reduce.4
  144.8 89.2 all-reduce.6
  247.3 37.0 all-reduce.8
  302.0 90.4 all-reduce.10
